TPU v7x, 32 devices: a whole 2x2x4 slice. The times are simulated.
32 devices in a mesh: section: 2 (over x), fsdp: 16 (over z, y, core).
Axes of the slice: x: 2, y: 2, z: 4, core: 2. Of those that a mesh axis runs over, the one named last changes fastest.
Arguments:
- history: bfloat16 [4, 16, 32, 2048], P(None, 'fsdp'), may hold values from -6 to 6
- keymask: int32 [4, 16, 32], P(None, 'fsdp'), may hold values from 0 to 1, as said below
- codes: int32 [4, 16, 16, 2], P(None, 'fsdp'), may hold values from 0 to 15
- plan_table: bfloat16 [16, 2048], replicated, may hold values from -6 to 6
- query_weights: bfloat16 [2, 2048, 1024], P('section', 'fsdp'), may hold values from -0.125 to 0.125
- output_weights: bfloat16 [2, 1024, 2048], P('section', 'fsdp'), may hold values from -0.75 to 0.75
- gains: float32 [2, 2048], P('section'), may hold values from 0.5 to 1.5
- cotangent: bfloat16 [4, 16, 32, 2048], P(None, 'fsdp'), may hold values from -6 to 6
Outputs:
- section_grads: bfloat16 [2, 4, 16, 32, 2048], P('section', None, 'fsdp')
- gain_grads: float32 [2, 2048], P('section')
Inputs may be any that keep to these rules, and one draw needn't show every extreme that they name: `keymask`: in each series the ones form one run that ends at the last position and covers at least a quarter of the 32 positions.
All inputs are finite; a program needn't handle non-finite values.
Results may differ from a plain program's by a relative error of at most 0.014.
Values may be sent and summed in bfloat16 or wider, within the bound.
No kernel may reach another device: no remote copies, remote signals or barrier semaphores. Data moves between devices by JAX's collectives and lax.ppermute only.
A program may use at most 64 MiB of HBM per device.

v0:
```python
import math
import jax
import jax.numpy as jnp
from jax import lax
from jax.sharding import PartitionSpec as P

HEADS = 8
EPSILON = 1e-05


def shifted(array, axis, by):
    size = lax.axis_size(axis)
    pairs = [(i, i + by) for i in range(size) if 0 <= i + by < size]
    return lax.ppermute(array, axis, pairs)


def rms_scale(inputs, gain_vector):
    return (
        inputs
        * lax.rsqrt(jnp.mean(inputs * inputs, axis=-1, keepdims=True) + EPSILON)
        * gain_vector
    )


def attend_layer(section_input, source, key_mask, query_weight, output_weight, gain_vector):
    series_count, seq_length, model_width = section_input.shape
    half_width = model_width // 2
    head_dim = half_width // HEADS
    head_shape = (series_count, seq_length, HEADS, head_dim)
    input_wide = section_input.astype(jnp.float32)
    normed = rms_scale(input_wide, gain_vector)
    normed_source = rms_scale(source.astype(jnp.float32), gain_vector)
    normed_rows = normed.astype(jnp.bfloat16).reshape(series_count * seq_length, model_width)
    query_flat = jnp.dot(normed_rows, query_weight, preferred_element_type=jnp.float32)
    queries = query_flat.astype(jnp.bfloat16).reshape(head_shape)
    key_rows = normed_source[..., :half_width].astype(jnp.bfloat16).reshape(head_shape)
    value_rows = normed_source[..., half_width:].astype(jnp.bfloat16).reshape(head_shape)
    scores = jnp.einsum(
        "bqhd,bkhd->bhqk", queries, key_rows, preferred_element_type=jnp.float32
    ) / math.sqrt(head_dim)
    raised = jnp.exp(scores) * key_mask.astype(jnp.float32)[:, None, None, :]
    probs = (raised / jnp.sum(raised, axis=-1, keepdims=True)).astype(jnp.bfloat16)
    mixed = jnp.einsum("bhqk,bkhd->bqhd", probs, value_rows, preferred_element_type=jnp.float32)
    mixed = mixed.astype(jnp.bfloat16).reshape(series_count * seq_length, half_width)
    update = jnp.dot(mixed, output_weight, preferred_element_type=jnp.float32)
    return (input_wide + update.reshape(series_count, seq_length, model_width)).astype(jnp.bfloat16)


def pick_slot(stack, slot):
    return lax.dynamic_index_in_dim(stack, slot, 0, False)


def place_slot(stack, slot, update, keep):
    previous = pick_slot(stack, slot)
    return lax.dynamic_update_index_in_dim(stack, jnp.where(keep, update, previous), slot, 0)


def on_device(history, keymask, codes, plan_table, query_weights, output_weights, gains, cotangent):
    section_index = lax.axis_index("section")
    section_count = lax.axis_size("section")
    half_sections = section_count // 2
    micro_count, series_count, seq_length, model_width = history.shape
    gathered_query, gathered_output = (
        lax.all_gather(query_weights, "fsdp", axis=1, tiled=True),
        lax.all_gather(output_weights, "fsdp", axis=1, tiled=True),
    )
    query_weight = gathered_query[0]
    output_weight = gathered_output[0]
    gain_vector = gains[0]
    code_rows = codes.reshape(micro_count, series_count, seq_length)
    code_count = plan_table.shape[0]
    one_hot = (code_rows[..., None] == jnp.arange(code_count, dtype=jnp.int32)).astype(jnp.bfloat16)
    plan_tokens = jnp.einsum(
        "msln,nd->msld", one_hot, plan_table, preferred_element_type=jnp.float32
    ).astype(jnp.bfloat16)
    is_decoder = section_index >= half_sections
    zero_act = jnp.zeros((series_count, seq_length, model_width), jnp.bfloat16)
    zero_stack = jnp.zeros(history.shape, jnp.bfloat16)
    tick_count = micro_count + section_count - 1

    def forward_tick(tick_index, state_tuple):
        got_input, got_memory, inputs_buf, memory_buf = state_tuple
        micro_index = tick_index - section_index
        is_active = (micro_index >= 0) & (micro_index < micro_count)
        slot = jnp.clip(micro_index, 0, micro_count - 1)
        key_mask = pick_slot(keymask, slot)
        section_input = jnp.where(
            section_index == 0,
            pick_slot(history, slot),
            jnp.where(section_index == half_sections, pick_slot(plan_tokens, slot), got_input),
        )
        memory = got_memory
        source = jnp.where(is_decoder, memory, section_input)

        def run_layer():
            return attend_layer(
                section_input, source, key_mask, query_weight, output_weight, gain_vector
            )

        def skip_layer():
            return zero_act

        output = lax.cond(is_active, run_layer, skip_layer)
        inputs_buf = place_slot(inputs_buf, slot, section_input, is_active)
        memory_buf = place_slot(memory_buf, slot, memory, is_active & is_decoder)
        outgoing = jnp.where(
            section_index == half_sections - 1, output, jnp.where(is_decoder, memory, zero_act)
        )
        got_input, got_memory = shifted((output, outgoing), "section", 1)
        return (got_input, got_memory, inputs_buf, memory_buf)

    start_state = (zero_act, zero_act, zero_stack, zero_stack)
    _, _, inputs_buf, memory_buf = lax.fori_loop(0, tick_count, forward_tick, start_state)

    def backward_tick(tick_index, state_tuple):
        got_grad, got_memory_grad, grads_buf, gain_total = state_tuple
        micro_index = tick_index - (section_count - 1 - section_index)
        is_active = (micro_index >= 0) & (micro_index < micro_count)
        slot = jnp.clip(micro_index, 0, micro_count - 1)
        key_mask = pick_slot(keymask, slot)
        out_grad = jnp.where(
            section_index == section_count - 1, pick_slot(cotangent, slot), got_grad
        )
        section_input = pick_slot(inputs_buf, slot)
        memory = pick_slot(memory_buf, slot)

        def section_map(layer_input, layer_memory, layer_gain):
            layer_source = jnp.where(is_decoder, layer_memory, layer_input)
            return attend_layer(
                layer_input, layer_source, key_mask, query_weight, output_weight, layer_gain
            )

        def run_grads():
            _, pull = jax.vjp(section_map, section_input, memory, gain_vector)
            return pull(out_grad)

        def skip_grads():
            return (zero_act, zero_act, jnp.zeros_like(gain_vector))

        input_grad, memory_grad, gain_grad = lax.cond(is_active, run_grads, skip_grads)
        memory_sum = jnp.where(is_decoder, got_memory_grad + memory_grad, zero_act)
        send_main = jnp.where(section_index == half_sections, memory_sum, input_grad)
        send_side = jnp.where(is_decoder & (section_index != half_sections), memory_sum, zero_act)
        got_grad, got_memory_grad = shifted((send_main, send_side), "section", -1)
        grads_buf = place_slot(grads_buf, slot, input_grad, is_active)
        gain_total = gain_total + lax.psum(gain_grad, "fsdp")
        return (got_grad, got_memory_grad, grads_buf, gain_total)

    back_state = (zero_act, zero_act, zero_stack, jnp.zeros_like(gain_vector))
    _, _, grads_buf, gain_total = lax.fori_loop(0, tick_count, backward_tick, back_state)
    return (grads_buf[None], gain_total[None])


def solution(mesh):
    return jax.shard_map(
        on_device,
        mesh=mesh,
        in_specs=(
            P(None, "fsdp", None, None),
            P(None, "fsdp", None),
            P(None, "fsdp", None, None),
            P(),
            P("section", "fsdp", None),
            P("section", "fsdp", None),
            P("section", None),
            P(None, "fsdp", None, None),
        ),
        out_specs=(P("section", None, "fsdp", None, None), P("section", None)),
        check_vma=False,
    )
```

profile of v0, /device:TPU:0, one launch (start us, length us, event | category | flops | bytes accessed | tf_op | source)
XLA Modules:
  0.0 415.8 jit_solution(3246150808287306456)
XLA Ops:
  9.9 53.6 %all-gather.3.cloned.1.call-done = bf16[1,1024,2048]{2,1,0:T(8,128)(2,1)} async-done(((bf16[1,64,2048]{2,1,0:T(8,128)(2,1)}), bf16[1,1024,2048]{2,1,0:T(8,128)(2,1)}) %all-gather.3.cloned.1.call-update) | async-done | bytes 4194320 | tf_op jit(solution)/shard_map/all_gather | solution.py:65
  63.5 51.2 %all-gather.5.cloned.1.call-done = bf16[1,2048,1024]{2,1,0:T(8,128)(2,1)} async-done(((bf16[1,128,1024]{2,1,0:T(8,128)(2,1)}), bf16[1,2048,1024]{2,1,0:T(8,128)(2,1)}) %all-gather.5.cloned.1.call-update) | async-done | bytes 4194320 | tf_op jit(solution)/shard_map/all_gather | solution.py:64
  114.9 89.8 %while.42 = (s32[]{:T(128)}, bf16[1,32,2048]{2,1,0:T(8,128)(2,1)S(1)}, bf16[1,32,2048]{2,1,0:T(8,128)(2,1)S(1)}, bf16[4,1,32,2048]{3,2,1,0:T(8,128)(2,1)S(1)}, b...) while((s32[]{:T(128)}, ...), condition=%wide.region_6.7_spmd, body=%wide.region_0.6_spmd.sunk | while | flops 274366848 | bytes 14173985 | solution.py:113
  114.9 1.0 bitcast_dynamic-update-slice_fusion.6
  116.0 8.3 %conditional.5 = (bf16[1,32,2048]{2,1,0:T(8,128)(2,1)S(1)}) conditional(s32[]{:T(128)} %convert_element_type.398, () %tuple.120, (bf16[1,32,2048]{2,1,0:T(8,128)(2,1)S(1)}, pred[1,32,2048]{2,1,0:T(8,128)(4,1)S(1)}, bf16[1,32,2048]{2,1,0:T(8,128)(2,1)S(1)}, f32[1,2048]{1,0:T(1,128)}, bf16[2048,1024]{1,0:T(8,128)(2,1)}, ...), branch_computations={%region_1.1_spmd, %region_2.5_spmd} | conditional | flops 273973632 | bytes 10700172 | solution.py:103
  117.0 3.1 fusion.5
  121.2 3.0 fusion.1
  124.3 1.3 collective-permute-start
  125.6 1.3 collective-permute-start.1
  127.0 4.8 %collective-permute-done.1 = bf16[1,32,2048]{2,1,0:T(8,128)(2,1)S(1)} collective-permute-done((bf16[1,32,2048]{2,1,0:T(8,128)(2,1)S(1)}, bf16[1,32,2048]{2,1,0:T(8,128)(2,1)S(1)}, u32[]{:S(2)}, u32[]{:S(2)}) %collective-permute-start.1) | collective-permute-done | bytes 131104 | tf_op jit(solution)/shard_map/while/body/eval_jaxpr/ppermute | solution.py:14
  132.9 8.3 %conditional.5 = (bf16[1,32,2048]{2,1,0:T(8,128)(2,1)S(1)}) conditional(s32[]{:T(128)} %convert_element_type.398, () %tuple.120, (bf16[1,32,2048]{2,1,0:T(8,128)(2,1)S(1)}, pred[1,32,2048]{2,1,0:T(8,128)(4,1)S(1)}, bf16[1,32,2048]{2,1,0:T(8,128)(2,1)S(1)}, f32[1,2048]{1,0:T(1,128)}, bf16[2048,1024]{1,0:T(8,128)(2,1)}, ...), branch_computations={%region_1.1_spmd, %region_2.5_spmd} | conditional | flops 273973632 | bytes 10700172 | solution.py:103
  134.0 3.1 fusion.5
  138.2 3.0 fusion.1
  141.2 4.4 %collective-permute-start = (bf16[1,32,2048]{2,1,0:T(8,128)(2,1)S(1)}, bf16[1,32,2048]{2,1,0:T(8,128)(2,1)S(1)}, u32[]{:S(2)}, u32[]{:S(2)}) collective-permute-start(bf16[1,32,2048]{2,1,0:T(8,128)(2,1)S(1)} %get-tuple-element.1286), channel_id=1, source_target_pairs={{0,16},{1,17},{2,18},{3,19},{4,20},{5,21},{6,22},{7,23},{8,24},{9,... | collective-permute-start | bytes 393224 | tf_op jit(solution)/shard_map/while/body/eval_jaxpr/ppermute | solution.py:14
  145.6 1.3 collective-permute-start.1
  147.0 4.0 collective-permute-done.1
  151.1 1.0 bitcast_dynamic-update-slice_fusion.6
  152.1 8.3 %conditional.5 = (bf16[1,32,2048]{2,1,0:T(8,128)(2,1)S(1)}) conditional(s32[]{:T(128)} %convert_element_type.398, () %tuple.120, (bf16[1,32,2048]{2,1,0:T(8,128)(2,1)S(1)}, pred[1,32,2048]{2,1,0:T(8,128)(4,1)S(1)}, bf16[1,32,2048]{2,1,0:T(8,128)(2,1)S(1)}, f32[1,2048]{1,0:T(1,128)}, bf16[2048,1024]{1,0:T(8,128)(2,1)}, ...), branch_computations={%region_1.1_spmd, %region_2.5_spmd} | conditional | flops 273973632 | bytes 10700172 | solution.py:103
  153.2 3.1 fusion.5
  157.4 3.0 fusion.1
  160.4 4.4 %collective-permute-start = (bf16[1,32,2048]{2,1,0:T(8,128)(2,1)S(1)}, bf16[1,32,2048]{2,1,0:T(8,128)(2,1)S(1)}, u32[]{:S(2)}, u32[]{:S(2)}) collective-permute-start(bf16[1,32,2048]{2,1,0:T(8,128)(2,1)S(1)} %get-tuple-element.1286), channel_id=1, source_target_pairs={{0,16},{1,17},{2,18},{3,19},{4,20},{5,21},{6,22},{7,23},{8,24},{9,... | collective-permute-start | bytes 393224 | tf_op jit(solution)/shard_map/while/body/eval_jaxpr/ppermute | solution.py:14
  164.8 1.3 collective-permute-start.1
  166.2 3.2 collective-permute-done.1
  170.5 8.3 %conditional.5 = (bf16[1,32,2048]{2,1,0:T(8,128)(2,1)S(1)}) conditional(s32[]{:T(128)} %convert_element_type.398, () %tuple.120, (bf16[1,32,2048]{2,1,0:T(8,128)(2,1)S(1)}, pred[1,32,2048]{2,1,0:T(8,128)(4,1)S(1)}, bf16[1,32,2048]{2,1,0:T(8,128)(2,1)S(1)}, f32[1,2048]{1,0:T(1,128)}, bf16[2048,1024]{1,0:T(8,128)(2,1)}, ...), branch_computations={%region_1.1_spmd, %region_2.5_spmd} | conditional | flops 273973632 | bytes 10700172 | solution.py:103
  171.5 3.1 fusion.5
  175.7 3.0 fusion.1
  178.8 4.4 %collective-permute-start = (bf16[1,32,2048]{2,1,0:T(8,128)(2,1)S(1)}, bf16[1,32,2048]{2,1,0:T(8,128)(2,1)S(1)}, u32[]{:S(2)}, u32[]{:S(2)}) collective-permute-start(bf16[1,32,2048]{2,1,0:T(8,128)(2,1)S(1)} %get-tuple-element.1286), channel_id=1, source_target_pairs={{0,16},{1,17},{2,18},{3,19},{4,20},{5,21},{6,22},{7,23},{8,24},{9,... | collective-permute-start | bytes 393224 | tf_op jit(solution)/shard_map/while/body/eval_jaxpr/ppermute | solution.py:14
  183.2 1.3 collective-permute-start.1
  184.6 2.5 collective-permute-done.1
  188.2 12.6 %collective-permute-start = (bf16[1,32,2048]{2,1,0:T(8,128)(2,1)S(1)}, bf16[1,32,2048]{2,1,0:T(8,128)(2,1)S(1)}, u32[]{:S(2)}, u32[]{:S(2)}) collective-permute-start(bf16[1,32,2048]{2,1,0:T(8,128)(2,1)S(1)} %get-tuple-element.1286), channel_id=1, source_target_pairs={{0,16},{1,17},{2,18},{3,19},{4,20},{5,21},{6,22},{7,23},{8,24},{9,... | collective-permute-start | bytes 393224 | tf_op jit(solution)/shard_map/while/body/eval_jaxpr/ppermute | solution.py:14
  200.8 1.3 collective-permute-start.1
  202.2 2.5 collective-permute-done.1
  204.8 203.3 %while.43 = (s32[]{:T(128)}, bf16[1,32,2048]{2,1,0:T(8,128)(2,1)S(1)}, bf16[1,32,2048]{2,1,0:T(8,128)(2,1)S(1)}, bf16[4,1,32,2048]{3,2,1,0:T(8,128)(2,1)S(1)}, f...) while((s32[]{:T(128)}, ...), condition=%wide.region_19.20_spmd.clone, body=%wide.region_7.19_spmd.clone.sunk | while | flops 417616544 | bytes 54182452 | solution.py:150
  205.0 1.3 collective-permute-start.2
  206.3 1.3 collective-permute-start.3
  207.6 30.0 %psum.15 = f32[2048]{0:T(1024)S(1)} all-reduce(f32[2048]{0:T(1024)S(1)} %get-tuple-element.1162), channel_id=1, replica_groups=mesh['section'=2,'fsdp'=16] {'fsdp'}, use_global_device_ids=true, to_apply=%region_18.18 | all-reduce | flops 2048 | bytes 16384 | tf_op jit(solution)/shard_map/while/body/eval_jaxpr/psum | solution.py:146
  237.8 9.8 %conditional.6 = (bf16[1,32,2048]{2,1,0:T(8,128)(2,1)S(1)}, bf16[1,32,2048]{2,1,0:T(8,128)(2,1)S(1)}, f32[2048]{0:T(1024)S(1)}) conditional(s32[]{:T(128)} %convert_element_type.399, () %tuple.124, (bf16[4,1,32,2048]{3,2,1,0:T(8,128)(2,1)S(1)}, s32[]{:T(128)}, pred[1,32,2048]{2,1,0:T(32,128)(4,1)S(1)}, bf16[1,32,2048]{2,1,0:T(8,128)(2,1)S(1)}, ...), branch_computations={%region_8.8_spmd, %region_9.17_spmd} | conditional | flops 417282720 | bytes 51716228 | solution.py:140
  239.0 3.1 fusion.38
  243.2 1.3 fusion.37
  245.7 1.5 fusion.50
  247.6 1.3 collective-permute-start.2
  248.9 1.3 collective-permute-start.3
  250.3 30.0 %psum.15 = f32[2048]{0:T(1024)S(1)} all-reduce(f32[2048]{0:T(1024)S(1)} %get-tuple-element.1162), channel_id=1, replica_groups=mesh['section'=2,'fsdp'=16] {'fsdp'}, use_global_device_ids=true, to_apply=%region_18.18 | all-reduce | flops 2048 | bytes 16384 | tf_op jit(solution)/shard_map/while/body/eval_jaxpr/psum | solution.py:146
  280.4 9.8 %conditional.6 = (bf16[1,32,2048]{2,1,0:T(8,128)(2,1)S(1)}, bf16[1,32,2048]{2,1,0:T(8,128)(2,1)S(1)}, f32[2048]{0:T(1024)S(1)}) conditional(s32[]{:T(128)} %convert_element_type.399, () %tuple.124, (bf16[4,1,32,2048]{3,2,1,0:T(8,128)(2,1)S(1)}, s32[]{:T(128)}, pred[1,32,2048]{2,1,0:T(32,128)(4,1)S(1)}, bf16[1,32,2048]{2,1,0:T(8,128)(2,1)S(1)}, ...), branch_computations={%region_8.8_spmd, %region_9.17_spmd} | conditional | flops 417282720 | bytes 51716228 | solution.py:140
  281.6 3.1 fusion.38
  285.8 1.3 fusion.37
  288.4 1.5 fusion.50
  290.2 1.3 collective-permute-start.2
  291.5 1.3 collective-permute-start.3
  292.9 30.0 %psum.15 = f32[2048]{0:T(1024)S(1)} all-reduce(f32[2048]{0:T(1024)S(1)} %get-tuple-element.1162), channel_id=1, replica_groups=mesh['section'=2,'fsdp'=16] {'fsdp'}, use_global_device_ids=true, to_apply=%region_18.18 | all-reduce | flops 2048 | bytes 16384 | tf_op jit(solution)/shard_map/while/body/eval_jaxpr/psum | solution.py:146
  323.0 9.8 %conditional.6 = (bf16[1,32,2048]{2,1,0:T(8,128)(2,1)S(1)}, bf16[1,32,2048]{2,1,0:T(8,128)(2,1)S(1)}, f32[2048]{0:T(1024)S(1)}) conditional(s32[]{:T(128)} %convert_element_type.399, () %tuple.124, (bf16[4,1,32,2048]{3,2,1,0:T(8,128)(2,1)S(1)}, s32[]{:T(128)}, pred[1,32,2048]{2,1,0:T(32,128)(4,1)S(1)}, bf16[1,32,2048]{2,1,0:T(8,128)(2,1)S(1)}, ...), branch_computations={%region_8.8_spmd, %region_9.17_spmd} | conditional | flops 417282720 | bytes 51716228 | solution.py:140
  324.2 3.1 fusion.38
  328.4 1.3 fusion.37
  331.0 1.5 fusion.50
  332.8 1.3 collective-permute-start.2
  334.1 1.3 collective-permute-start.3
  335.5 30.0 %psum.15 = f32[2048]{0:T(1024)S(1)} all-reduce(f32[2048]{0:T(1024)S(1)} %get-tuple-element.1162), channel_id=1, replica_groups=mesh['section'=2,'fsdp'=16] {'fsdp'}, use_global_device_ids=true, to_apply=%region_18.18 | all-reduce | flops 2048 | bytes 16384 | tf_op jit(solution)/shard_map/while/body/eval_jaxpr/psum | solution.py:146
  365.6 9.8 %conditional.6 = (bf16[1,32,2048]{2,1,0:T(8,128)(2,1)S(1)}, bf16[1,32,2048]{2,1,0:T(8,128)(2,1)S(1)}, f32[2048]{0:T(1024)S(1)}) conditional(s32[]{:T(128)} %convert_element_type.399, () %tuple.124, (bf16[4,1,32,2048]{3,2,1,0:T(8,128)(2,1)S(1)}, s32[]{:T(128)}, pred[1,32,2048]{2,1,0:T(32,128)(4,1)S(1)}, bf16[1,32,2048]{2,1,0:T(8,128)(2,1)S(1)}, ...), branch_computations={%region_8.8_spmd, %region_9.17_spmd} | conditional | flops 417282720 | bytes 51716228 | solution.py:140
  366.8 3.1 fusion.38
  371.0 1.3 fusion.37
  373.6 1.5 fusion.50
  375.4 1.3 collective-permute-start.2
  376.7 1.3 collective-permute-start.3
  378.1 30.0 %psum.15 = f32[2048]{0:T(1024)S(1)} all-reduce(f32[2048]{0:T(1024)S(1)} %get-tuple-element.1162), channel_id=1, replica_groups=mesh['section'=2,'fsdp'=16] {'fsdp'}, use_global_device_ids=true, to_apply=%region_18.18 | all-reduce | flops 2048 | bytes 16384 | tf_op jit(solution)/shard_map/while/body/eval_jaxpr/psum | solution.py:146
  (262 shorter events, 31.0 us)
Async XLA Ops:
  7.2 2.4 copy-start
  7.2 56.3 %all-gather.3.cloned.1.call-start = ((), (), s32[]{:S(2)}) async-start(), calls=%async_computation | async-start | bytes 4456448 | tf_op jit(solution)/shard_map/all_gather | solution.py:65
  7.9 106.8 %all-gather.5.cloned.1.call-start = ((), (), s32[]{:S(2)}) async-start(), calls=%async_computation.1 | async-start | bytes 4456448 | tf_op jit(solution)/shard_map/all_gather | solution.py:64
  114.9 89.9 %copy-start.4 = (bf16[4,1,32,2048]{3,2,1,0:T(8,128)(2,1)S(1)}, bf16[4,1,32,2048]{3,2,1,0:T(8,128)(2,1)}, u32[]{:S(2)}) copy-start(bf16[4,1,32,2048]{3,2,1,0:T(8,128)(2,1)} %param.23) | copy-start | bytes 1572868
  124.3 7.6 %collective-permute-start = (bf16[1,32,2048]{2,1,0:T(8,128)(2,1)S(1)}, bf16[1,32,2048]{2,1,0:T(8,128)(2,1)S(1)}, u32[]{:S(2)}, u32[]{:S(2)}) collective-permute-start(bf16[1,32,2048]{2,1,0:T(8,128)(2,1)S(1)} %get-tuple-element.1286), channel_id=1, source_target_pairs={{0,16},{1,17},{2,18},{3,19},{4,20},{5,21},{6,22},{7,23},{8,24},{9,... | collective-permute-start | bytes 393224 | tf_op jit(solution)/shard_map/while/body/eval_jaxpr/ppermute | solution.py:14
  125.6 6.2 %collective-permute-start.1 = (bf16[1,32,2048]{2,1,0:T(8,128)(2,1)S(1)}, bf16[1,32,2048]{2,1,0:T(8,128)(2,1)S(1)}, u32[]{:S(2)}, u32[]{:S(2)}) collective-permute-start(bf16[1,32,2048]{2,1,0:T(8,128)(2,1)S(1)} %select_select_fusion.2), channel_id=1, source_target_pairs={{0,16},{1,17},{2,18},{3,19},{4,20},{5,21},{6,22},{7,23},{8,24},{9,... | collective-permute-start | bytes 393224 | tf_op jit(solution)/shard_map/while/body/eval_jaxpr/ppermute | solution.py:14
  141.2 9.9 %collective-permute-start = (bf16[1,32,2048]{2,1,0:T(8,128)(2,1)S(1)}, bf16[1,32,2048]{2,1,0:T(8,128)(2,1)S(1)}, u32[]{:S(2)}, u32[]{:S(2)}) collective-permute-start(bf16[1,32,2048]{2,1,0:T(8,128)(2,1)S(1)} %get-tuple-element.1286), channel_id=1, source_target_pairs={{0,16},{1,17},{2,18},{3,19},{4,20},{5,21},{6,22},{7,23},{8,24},{9,... | collective-permute-start | bytes 393224 | tf_op jit(solution)/shard_map/while/body/eval_jaxpr/ppermute | solution.py:14
  145.6 5.4 %collective-permute-start.1 = (bf16[1,32,2048]{2,1,0:T(8,128)(2,1)S(1)}, bf16[1,32,2048]{2,1,0:T(8,128)(2,1)S(1)}, u32[]{:S(2)}, u32[]{:S(2)}) collective-permute-start(bf16[1,32,2048]{2,1,0:T(8,128)(2,1)S(1)} %select_select_fusion.2), channel_id=1, source_target_pairs={{0,16},{1,17},{2,18},{3,19},{4,20},{5,21},{6,22},{7,23},{8,24},{9,... | collective-permute-start | bytes 393224 | tf_op jit(solution)/shard_map/while/body/eval_jaxpr/ppermute | solution.py:14
  160.4 9.0 %collective-permute-start = (bf16[1,32,2048]{2,1,0:T(8,128)(2,1)S(1)}, bf16[1,32,2048]{2,1,0:T(8,128)(2,1)S(1)}, u32[]{:S(2)}, u32[]{:S(2)}) collective-permute-start(bf16[1,32,2048]{2,1,0:T(8,128)(2,1)S(1)} %get-tuple-element.1286), channel_id=1, source_target_pairs={{0,16},{1,17},{2,18},{3,19},{4,20},{5,21},{6,22},{7,23},{8,24},{9,... | collective-permute-start | bytes 393224 | tf_op jit(solution)/shard_map/while/body/eval_jaxpr/ppermute | solution.py:14
  164.8 4.5 %collective-permute-start.1 = (bf16[1,32,2048]{2,1,0:T(8,128)(2,1)S(1)}, bf16[1,32,2048]{2,1,0:T(8,128)(2,1)S(1)}, u32[]{:S(2)}, u32[]{:S(2)}) collective-permute-start(bf16[1,32,2048]{2,1,0:T(8,128)(2,1)S(1)} %select_select_fusion.2), channel_id=1, source_target_pairs={{0,16},{1,17},{2,18},{3,19},{4,20},{5,21},{6,22},{7,23},{8,24},{9,... | collective-permute-start | bytes 393224 | tf_op jit(solution)/shard_map/while/body/eval_jaxpr/ppermute | solution.py:14
  178.8 8.3 %collective-permute-start = (bf16[1,32,2048]{2,1,0:T(8,128)(2,1)S(1)}, bf16[1,32,2048]{2,1,0:T(8,128)(2,1)S(1)}, u32[]{:S(2)}, u32[]{:S(2)}) collective-permute-start(bf16[1,32,2048]{2,1,0:T(8,128)(2,1)S(1)} %get-tuple-element.1286), channel_id=1, source_target_pairs={{0,16},{1,17},{2,18},{3,19},{4,20},{5,21},{6,22},{7,23},{8,24},{9,... | collective-permute-start | bytes 393224 | tf_op jit(solution)/shard_map/while/body/eval_jaxpr/ppermute | solution.py:14
  183.2 3.8 collective-permute-start.1
  188.2 16.5 %collective-permute-start = (bf16[1,32,2048]{2,1,0:T(8,128)(2,1)S(1)}, bf16[1,32,2048]{2,1,0:T(8,128)(2,1)S(1)}, u32[]{:S(2)}, u32[]{:S(2)}) collective-permute-start(bf16[1,32,2048]{2,1,0:T(8,128)(2,1)S(1)} %get-tuple-element.1286), channel_id=1, source_target_pairs={{0,16},{1,17},{2,18},{3,19},{4,20},{5,21},{6,22},{7,23},{8,24},{9,... | collective-permute-start | bytes 393224 | tf_op jit(solution)/shard_map/while/body/eval_jaxpr/ppermute | solution.py:14
  200.8 3.8 collective-permute-start.1
  205.0 32.7 %collective-permute-start.2 = (bf16[1,32,2048]{2,1,0:T(8,128)(2,1)S(1)}, bf16[1,32,2048]{2,1,0:T(8,128)(2,1)S(1)}, u32[]{:S(2)}, u32[]{:S(2)}) collective-permute-start(bf16[1,32,2048]{2,1,0:T(8,128)(2,1)S(1)} %get-tuple-element.1160), channel_id=1, source_target_pairs={{16,0},{17,1},{18,2},{19,3},{20,4},{21,5},{22,6},{23,7},{24,8},{25... | collective-permute-start | bytes 393224 | tf_op jit(solution)/shard_map/while/body/eval_jaxpr/ppermute | solution.py:14
  206.3 31.4 %collective-permute-start.3 = (bf16[1,32,2048]{2,1,0:T(8,128)(2,1)S(1)}, bf16[1,32,2048]{2,1,0:T(8,128)(2,1)S(1)}, u32[]{:S(2)}, u32[]{:S(2)}) collective-permute-start(bf16[1,32,2048]{2,1,0:T(8,128)(2,1)S(1)} %get-tuple-element.1161), channel_id=1, source_target_pairs={{16,0},{17,1},{18,2},{19,3},{20,4},{21,5},{22,6},{23,7},{24,8},{25... | collective-permute-start | bytes 393224 | tf_op jit(solution)/shard_map/while/body/eval_jaxpr/ppermute | solution.py:14
  237.8 5.4 %copy-start.2 = (bf16[1024,2048]{1,0:T(8,128)(2,1)S(1)}, bf16[1024,2048]{1,0:T(8,128)(2,1)}, u32[]{:S(2)}) copy-start(bf16[1024,2048]{1,0:T(8,128)(2,1)} %get-tuple-element.750) | copy-start | bytes 12582916 | tf_op jit(solution)/shard_map/while/body/eval_jaxpr/cond
  242.1 3.1 copy-start.3
  242.1 3.6 copy-start.1
  247.6 32.7 %collective-permute-start.2 = (bf16[1,32,2048]{2,1,0:T(8,128)(2,1)S(1)}, bf16[1,32,2048]{2,1,0:T(8,128)(2,1)S(1)}, u32[]{:S(2)}, u32[]{:S(2)}) collective-permute-start(bf16[1,32,2048]{2,1,0:T(8,128)(2,1)S(1)} %get-tuple-element.1160), channel_id=1, source_target_pairs={{16,0},{17,1},{18,2},{19,3},{20,4},{21,5},{22,6},{23,7},{24,8},{25... | collective-permute-start | bytes 393224 | tf_op jit(solution)/shard_map/while/body/eval_jaxpr/ppermute | solution.py:14
  248.9 31.4 %collective-permute-start.3 = (bf16[1,32,2048]{2,1,0:T(8,128)(2,1)S(1)}, bf16[1,32,2048]{2,1,0:T(8,128)(2,1)S(1)}, u32[]{:S(2)}, u32[]{:S(2)}) collective-permute-start(bf16[1,32,2048]{2,1,0:T(8,128)(2,1)S(1)} %get-tuple-element.1161), channel_id=1, source_target_pairs={{16,0},{17,1},{18,2},{19,3},{20,4},{21,5},{22,6},{23,7},{24,8},{25... | collective-permute-start | bytes 393224 | tf_op jit(solution)/shard_map/while/body/eval_jaxpr/ppermute | solution.py:14
  280.4 5.4 %copy-start.2 = (bf16[1024,2048]{1,0:T(8,128)(2,1)S(1)}, bf16[1024,2048]{1,0:T(8,128)(2,1)}, u32[]{:S(2)}) copy-start(bf16[1024,2048]{1,0:T(8,128)(2,1)} %get-tuple-element.750) | copy-start | bytes 12582916 | tf_op jit(solution)/shard_map/while/body/eval_jaxpr/cond
  284.7 3.1 copy-start.3
  284.8 3.6 copy-start.1
  290.2 32.7 %collective-permute-start.2 = (bf16[1,32,2048]{2,1,0:T(8,128)(2,1)S(1)}, bf16[1,32,2048]{2,1,0:T(8,128)(2,1)S(1)}, u32[]{:S(2)}, u32[]{:S(2)}) collective-permute-start(bf16[1,32,2048]{2,1,0:T(8,128)(2,1)S(1)} %get-tuple-element.1160), channel_id=1, source_target_pairs={{16,0},{17,1},{18,2},{19,3},{20,4},{21,5},{22,6},{23,7},{24,8},{25... | collective-permute-start | bytes 393224 | tf_op jit(solution)/shard_map/while/body/eval_jaxpr/ppermute | solution.py:14
  291.5 31.4 %collective-permute-start.3 = (bf16[1,32,2048]{2,1,0:T(8,128)(2,1)S(1)}, bf16[1,32,2048]{2,1,0:T(8,128)(2,1)S(1)}, u32[]{:S(2)}, u32[]{:S(2)}) collective-permute-start(bf16[1,32,2048]{2,1,0:T(8,128)(2,1)S(1)} %get-tuple-element.1161), channel_id=1, source_target_pairs={{16,0},{17,1},{18,2},{19,3},{20,4},{21,5},{22,6},{23,7},{24,8},{25... | collective-permute-start | bytes 393224 | tf_op jit(solution)/shard_map/while/body/eval_jaxpr/ppermute | solution.py:14
  323.0 5.4 %copy-start.2 = (bf16[1024,2048]{1,0:T(8,128)(2,1)S(1)}, bf16[1024,2048]{1,0:T(8,128)(2,1)}, u32[]{:S(2)}) copy-start(bf16[1024,2048]{1,0:T(8,128)(2,1)} %get-tuple-element.750) | copy-start | bytes 12582916 | tf_op jit(solution)/shard_map/while/body/eval_jaxpr/cond
  327.4 3.1 copy-start.3
  327.4 3.6 copy-start.1
  332.8 32.7 %collective-permute-start.2 = (bf16[1,32,2048]{2,1,0:T(8,128)(2,1)S(1)}, bf16[1,32,2048]{2,1,0:T(8,128)(2,1)S(1)}, u32[]{:S(2)}, u32[]{:S(2)}) collective-permute-start(bf16[1,32,2048]{2,1,0:T(8,128)(2,1)S(1)} %get-tuple-element.1160), channel_id=1, source_target_pairs={{16,0},{17,1},{18,2},{19,3},{20,4},{21,5},{22,6},{23,7},{24,8},{25... | collective-permute-start | bytes 393224 | tf_op jit(solution)/shard_map/while/body/eval_jaxpr/ppermute | solution.py:14
  334.1 31.4 %collective-permute-start.3 = (bf16[1,32,2048]{2,1,0:T(8,128)(2,1)S(1)}, bf16[1,32,2048]{2,1,0:T(8,128)(2,1)S(1)}, u32[]{:S(2)}, u32[]{:S(2)}) collective-permute-start(bf16[1,32,2048]{2,1,0:T(8,128)(2,1)S(1)} %get-tuple-element.1161), channel_id=1, source_target_pairs={{16,0},{17,1},{18,2},{19,3},{20,4},{21,5},{22,6},{23,7},{24,8},{25... | collective-permute-start | bytes 393224 | tf_op jit(solution)/shard_map/while/body/eval_jaxpr/ppermute | solution.py:14
  365.6 5.4 %copy-start.2 = (bf16[1024,2048]{1,0:T(8,128)(2,1)S(1)}, bf16[1024,2048]{1,0:T(8,128)(2,1)}, u32[]{:S(2)}) copy-start(bf16[1024,2048]{1,0:T(8,128)(2,1)} %get-tuple-element.750) | copy-start | bytes 12582916 | tf_op jit(solution)/shard_map/while/body/eval_jaxpr/cond
  370.0 3.1 copy-start.3
  370.0 3.6 copy-start.1
  375.4 32.7 %collective-permute-start.2 = (bf16[1,32,2048]{2,1,0:T(8,128)(2,1)S(1)}, bf16[1,32,2048]{2,1,0:T(8,128)(2,1)S(1)}, u32[]{:S(2)}, u32[]{:S(2)}) collective-permute-start(bf16[1,32,2048]{2,1,0:T(8,128)(2,1)S(1)} %get-tuple-element.1160), channel_id=1, source_target_pairs={{16,0},{17,1},{18,2},{19,3},{20,4},{21,5},{22,6},{23,7},{24,8},{25... | collective-permute-start | bytes 393224 | tf_op jit(solution)/shard_map/while/body/eval_jaxpr/ppermute | solution.py:14
  376.7 31.4 %collective-permute-start.3 = (bf16[1,32,2048]{2,1,0:T(8,128)(2,1)S(1)}, bf16[1,32,2048]{2,1,0:T(8,128)(2,1)S(1)}, u32[]{:S(2)}, u32[]{:S(2)}) collective-permute-start(bf16[1,32,2048]{2,1,0:T(8,128)(2,1)S(1)} %get-tuple-element.1161), channel_id=1, source_target_pairs={{16,0},{17,1},{18,2},{19,3},{20,4},{21,5},{22,6},{23,7},{24,8},{25... | collective-permute-start | bytes 393224 | tf_op jit(solution)/shard_map/while/body/eval_jaxpr/ppermute | solution.py:14
  408.2 0.8 copy-start.5
  408.2 0.8 copy-start.6
Sparse Core Ops, SparseCore 0:
  10.2 53.2 all-gather.2
  65.6 49.0 all-gather.4
where the time goes:
time: 417 us; the launch traced here: 416 us
  blocking collectives  150 us (36%)
  waiting for transfers between devices  123 us (29%)
  matrix products  54.3 us (13%)
  starting transfers between devices  46.6 us (11%)
  other arithmetic  22.1 us (5%)
  between operations  14.2 us (3%)
    psum x5, blocking collectives, backward_tick(): gain_total = gain_total + lax.psum(gain_grad, 'fsdp')  150 us
    all_gather x1, waiting for transfers between devices, on_device(): lax.all_gather(output_weights, 'fsdp', axis=1, tiled=True)  53.6 us
    all_gather x1, waiting for transfers between devices, on_device(): lax.all_gather(query_weights, 'fsdp', axis=1, tiled=True)  51.2 us
    ppermute x20, starting transfers between devices, shifted(): return lax.ppermute(array, axis, pairs)  46.5 us
    dot_general x12, matrix products, attend_layer(): jnp.dot(normed_rows, query_weight, preferred_element_type=jnp.float32)  30.8 us
    dot_general x8, matrix products, attend_layer(): update = jnp.dot(mixed, output_weight, preferred_element_type=jnp.float32)  17.4 us
    ppermute x20, waiting for transfers between devices, shifted(): return lax.ppermute(array, axis, pairs)  17 us
  transfers between devices with their start and end apart: 22, of which 7 were waited for; matrix products, arithmetic and copies ran while one was open for 0% of the time, Pallas kernels for 0%

commit v1 on v0

--- a/solution.py
+++ b/solution.py
@@ -6,6 +6,28 @@
 
 HEADS = 8
 EPSILON = 1e-05
+
+
+def joined_along(tiles, dim):
+    lengths = list(tiles.shape[1:])
+    lengths[dim] *= tiles.shape[0]
+    return jnp.moveaxis(tiles, 0, dim).reshape(lengths)
+
+
+def gather_around(array, axis, dim):
+    peers = lax.axis_size(axis)
+    pairs = [(i, (i + 1) % peers) for i in range(peers)]
+    back = [(b, a) for a, b in pairs]
+    lower, upper = ([], [])
+    for step in range(peers - 1):
+        if step % 2 == 0:
+            lower.append(lax.ppermute(lower[-1] if lower else array, axis, pairs))
+        else:
+            upper.append(lax.ppermute(upper[-1] if upper else array, axis, back))
+    tiles = jnp.stack([*lower[::-1], array, *upper])
+    shift = lax.axis_index(axis) - len(lower)
+    tiles = tiles[(jnp.arange(peers) - shift) % peers]
+    return joined_along(tiles, dim)
 
 
 def shifted(array, axis, by):
@@ -61,7 +83,7 @@
     half_sections = section_count // 2
     micro_count, series_count, seq_length, model_width = history.shape
     gathered_query, gathered_output = (
-        lax.all_gather(query_weights, "fsdp", axis=1, tiled=True),
+        gather_around(query_weights, "fsdp", 1),
         lax.all_gather(output_weights, "fsdp", axis=1, tiled=True),
     )
     query_weight = gathered_query[0]

time: 417 us -> 383 us (0.918)
  waiting for transfers between devices: 123 us -> 58.2 us
  starting transfers between devices: 46.6 us -> 78 us
  other arithmetic: 22.1 us -> 10.2 us
  local copies, waits for them, and re-layouts: 3.25 us -> 14.3 us
    all_gather x1, waiting for transfers between devices: 53.6 us -> 0.01 us  [on_device(): lax.all_gather(output_weights, 'fsdp', axis=1, tiled=True)]
    all_gather x1 -> x0, waiting for transfers between devices: 51.2 us -> none  [on_device(): lax.all_gather(query_weights, 'fsdp', axis=1, tiled=True)]
    ppermute x0 -> x15, waiting for transfers between devices: none -> 45.2 us  [the longest x8 28.4 us: gather_around(): lower.append(lax.ppermute(lower[-1] if lower else array, axis, pairs))]
    ppermute x0 -> x15, starting transfers between devices: none -> 32.8 us  [the longest x7 32.3 us: gather_around(): upper.append(lax.ppermute(upper[-1] if upper else array, axis, back))]
    another operation x8, other arithmetic: 6.99 us -> 0.81 us
    unnamed x9 -> x34, local copies, waits for them, and re-layouts: 1.58 us -> 7.65 us
    convert_element_type x8, other arithmetic: 5.91 us -> 0.07 us  [attend_layer(): raised = jnp.exp(scores) * key_mask.astype(jnp.float32)[:, None, None, :]]
    gather x0 -> x1, local copies, waits for them, and re-layouts: none -> 5.01 us  [gather_around(): tiles = tiles[(jnp.arange(peers) - shift) % peers]]
  transfers between devices with their start and end apart: 22 -> 36, of which waited for: 7 -> 19; matrix products, arithmetic and copies ran while one was open for 0% -> 3% of each run, Pallas kernels for 0% -> 0%
where the time goes in v1:
time: 383 us; the launch traced here: 382 us
  blocking collectives  150 us (39%)
  starting transfers between devices  78 us (20%)
  waiting for transfers between devices  58.2 us (15%)
  matrix products  54.7 us (14%)
  local copies, waits for them, and re-layouts  14.3 us (4%)
  between operations  14.3 us (4%)
  other arithmetic  10.2 us (3%)
    psum x5, blocking collectives, backward_tick(): gain_total = gain_total + lax.psum(gain_grad, 'fsdp')  150 us
    ppermute x20, starting transfers between devices, shifted(): return lax.ppermute(array, axis, pairs)  45.2 us
    ppermute x7, starting transfers between devices, gather_around(): upper.append(lax.ppermute(upper[-1] if upper else array, axis, back))  32.3 us
    dot_general x12, matrix products, attend_layer(): jnp.dot(normed_rows, query_weight, preferred_element_type=jnp.float32)  31.2 us
    ppermute x8, waiting for transfers between devices, gather_around(): lower.append(lax.ppermute(lower[-1] if lower else array, axis, pairs))  28.4 us
    dot_general x8, matrix products, attend_layer(): update = jnp.dot(mixed, output_weight, preferred_element_type=jnp.float32)  17.4 us
    ppermute x7, waiting for transfers between devices, gather_around(): upper.append(lax.ppermute(upper[-1] if upper else array, axis, back))  16.8 us
    ppermute x20, waiting for transfers between devices, shifted(): return lax.ppermute(array, axis, pairs)  12.3 us
  transfers between devices with their start and end apart: 36, of which 19 were waited for; matrix products, arithmetic and copies ran while one was open for 3% of the time, Pallas kernels for 0%

profile of v1, /device:TPU:0, one launch (start us, length us, event | category | flops | bytes accessed | tf_op | source)
XLA Modules:
  0.0 382.0 jit_solution(10761594153587413024)
XLA Ops:
  8.4 9.3 %collective-permute-done.4 = bf16[1,128,1024]{2,1,0:T(8,128)(2,1)S(1)} collective-permute-done((bf16[1,128,1024]{2,1,0:T(8,128)(2,1)}, bf16[1,128,1024]{2,1,0:T(8,128)(2,1)S(1)}, u32[]{:S(2)}, u32[]{:S(2)}) %collective-permute-start.4) | collective-permute-done | bytes 262176 | tf_op jit(solution)/shard_map/ppermute | solution.py:24
  17.7 4.4 %collective-permute-start.12 = (bf16[1,128,1024]{2,1,0:T(8,128)(2,1)}, bf16[1,128,1024]{2,1,0:T(8,128)(2,1)S(1)}, u32[]{:S(2)}, u32[]{:S(2)}) collective-permute-start(bf16[1,128,1024]{2,1,0:T(8,128)(2,1)} %param.20), channel_id=1, source_target_pairs={{1,0},{2,1},{3,2},{4,3},{5,4},{6,5},{7,6},{8,7},{9,8},{10,9},{11,1... | collective-permute-start | bytes 786440 | tf_op jit(solution)/shard_map/ppermute | solution.py:26
  22.1 4.3 %collective-permute-done.5 = bf16[1,128,1024]{2,1,0:T(8,128)(2,1)S(1)} collective-permute-done((bf16[1,128,1024]{2,1,0:T(8,128)(2,1)S(1)}, bf16[1,128,1024]{2,1,0:T(8,128)(2,1)S(1)}, u32[]{:S(2)}, u32[]{:S(2)}) %collective-permute-start.5) | collective-permute-done | bytes 262176 | tf_op jit(solution)/shard_map/ppermute | solution.py:24
  27.3 4.6 %collective-permute-start.13 = (bf16[1,128,1024]{2,1,0:T(8,128)(2,1)S(1)}, bf16[1,128,1024]{2,1,0:T(8,128)(2,1)S(1)}, u32[]{:S(2)}, u32[]{:S(2)}) collective-permute-start(bf16[1,128,1024]{2,1,0:T(8,128)(2,1)S(1)} %collective-permute-done.12), channel_id=1, source_target_pairs={{1,0},{2,1},{3,2},{4,3},{5,4},{6,5},{7,6},{8,7},{9,8},{10,9},{11,1... | collective-permute-start | bytes 786440 | tf_op jit(solution)/shard_map/ppermute | solution.py:26
  31.9 4.5 %collective-permute-done.6 = bf16[1,128,1024]{2,1,0:T(8,128)(2,1)S(1)} collective-permute-done((bf16[1,128,1024]{2,1,0:T(8,128)(2,1)S(1)}, bf16[1,128,1024]{2,1,0:T(8,128)(2,1)S(1)}, u32[]{:S(2)}, u32[]{:S(2)}) %collective-permute-start.6) | collective-permute-done | bytes 262176 | tf_op jit(solution)/shard_map/ppermute | solution.py:24
  37.5 4.7 %collective-permute-start.14 = (bf16[1,128,1024]{2,1,0:T(8,128)(2,1)S(1)}, bf16[1,128,1024]{2,1,0:T(8,128)(2,1)S(1)}, u32[]{:S(2)}, u32[]{:S(2)}) collective-permute-start(bf16[1,128,1024]{2,1,0:T(8,128)(2,1)S(1)} %collective-permute-done.13), channel_id=1, source_target_pairs={{1,0},{2,1},{3,2},{4,3},{5,4},{6,5},{7,6},{8,7},{9,8},{10,9},{11,1... | collective-permute-start | bytes 786440 | tf_op jit(solution)/shard_map/ppermute | solution.py:26
  42.2 2.8 collective-permute-done.7
  45.0 5.9 %collective-permute-done.14 = bf16[1,128,1024]{2,1,0:T(8,128)(2,1)S(1)} collective-permute-done((bf16[1,128,1024]{2,1,0:T(8,128)(2,1)S(1)}, bf16[1,128,1024]{2,1,0:T(8,128)(2,1)S(1)}, u32[]{:S(2)}, u32[]{:S(2)}) %collective-permute-start.14) | collective-permute-done | bytes 262176 | tf_op jit(solution)/shard_map/ppermute | solution.py:26
  50.8 4.6 %collective-permute-start.15 = (bf16[1,128,1024]{2,1,0:T(8,128)(2,1)S(1)}, bf16[1,128,1024]{2,1,0:T(8,128)(2,1)S(1)}, u32[]{:S(2)}, u32[]{:S(2)}) collective-permute-start(bf16[1,128,1024]{2,1,0:T(8,128)(2,1)S(1)} %collective-permute-done.14), channel_id=1, source_target_pairs={{1,0},{2,1},{3,2},{4,3},{5,4},{6,5},{7,6},{8,7},{9,8},{10,9},{11,1... | collective-permute-start | bytes 786440 | tf_op jit(solution)/shard_map/ppermute | solution.py:26
  55.4 3.6 collective-permute-done.8
  59.8 4.7 %collective-permute-start.16 = (bf16[1,128,1024]{2,1,0:T(8,128)(2,1)S(1)}, bf16[1,128,1024]{2,1,0:T(8,128)(2,1)S(1)}, u32[]{:S(2)}, u32[]{:S(2)}) collective-permute-start(bf16[1,128,1024]{2,1,0:T(8,128)(2,1)S(1)} %collective-permute-done.15), channel_id=1, source_target_pairs={{1,0},{2,1},{3,2},{4,3},{5,4},{6,5},{7,6},{8,7},{9,8},{10,9},{11,1... | collective-permute-start | bytes 786440 | tf_op jit(solution)/shard_map/ppermute | solution.py:26
  64.4 3.2 collective-permute-done.9
  67.6 5.9 %collective-permute-done.16 = bf16[1,128,1024]{2,1,0:T(8,128)(2,1)S(1)} collective-permute-done((bf16[1,128,1024]{2,1,0:T(8,128)(2,1)S(1)}, bf16[1,128,1024]{2,1,0:T(8,128)(2,1)S(1)}, u32[]{:S(2)}, u32[]{:S(2)}) %collective-permute-start.16) | collective-permute-done | bytes 262176 | tf_op jit(solution)/shard_map/ppermute | solution.py:26
  73.5 4.6 %collective-permute-start.17 = (bf16[1,128,1024]{2,1,0:T(8,128)(2,1)S(1)}, bf16[1,128,1024]{2,1,0:T(8,128)(2,1)}, u32[]{:S(2)}, u32[]{:S(2)}) collective-permute-start(bf16[1,128,1024]{2,1,0:T(8,128)(2,1)S(1)} %collective-permute-done.16), channel_id=1, source_target_pairs={{1,0},{2,1},{3,2},{4,3},{5,4},{6,5},{7,6},{8,7},{9,8},{10,9},{11,1... | collective-permute-start | bytes 786440 | tf_op jit(solution)/shard_map/ppermute | solution.py:26
  79.6 2.4 collective-permute-done.17
  82.0 4.7 %collective-permute-start.18 = (bf16[1,128,1024]{2,1,0:T(8,128)(2,1)}, bf16[1,128,1024]{2,1,0:T(8,128)(2,1)S(1)}, u32[]{:S(2)}, u32[]{:S(2)}) collective-permute-start(bf16[1,128,1024]{2,1,0:T(8,128)(2,1)} %collective-permute-done.17), channel_id=1, source_target_pairs={{1,0},{2,1},{3,2},{4,3},{5,4},{6,5},{7,6},{8,7},{9,8},{10,9},{11,1... | collective-permute-start | bytes 786440 | tf_op jit(solution)/shard_map/ppermute | solution.py:26
  91.4 2.0 copy-done.4
  93.4 5.0 %gather_fusion = bf16[16,128,1024]{2,1,0:T(8,128)(2,1)} fusion(bf16[16,128,1024]{2,1,0:T(8,128)(2,1)} %bitcast.261, s32[1024]{0:T(1024)S(1)} %pad_clamp_fusion), kind=kCustom, calls=%fused_computation | custom fusion | bytes 8388672 | tf_op jit(solution)/shard_map/gather | solution.py:29
  98.6 78.4 %while.42 = (s32[]{:T(128)}, bf16[1,32,2048]{2,1,0:T(8,128)(2,1)S(1)}, bf16[1,32,2048]{2,1,0:T(8,128)(2,1)S(1)}, bf16[4,1,32,2048]{3,2,1,0:T(8,128)(2,1)S(1)}, b...) while((s32[]{:T(128)}, ...), condition=%wide.region_6.7_spmd, body=%wide.region_0.6_spmd.sunk | while | flops 274366848 | bytes 14173985 | solution.py:135
  99.7 6.9 %conditional.5 = (bf16[1,32,2048]{2,1,0:T(8,128)(2,1)S(1)}) conditional(s32[]{:T(128)} %convert_element_type.398, () %tuple.120, (bf16[1,32,2048]{2,1,0:T(8,128)(2,1)S(1)}, pred[1,32,2048]{2,1,0:T(8,128)(4,1)S(1)}, bf16[1,32,2048]{2,1,0:T(8,128)(2,1)S(1)}, f32[1,2048]{1,0:T(1,128)S(1)}, bf16[2048,1024]{1,0:T(8,128)(2,1)}, ...), branch_computations={%region_1.1_spmd, %region_2.5_spmd} | conditional | flops 273973632 | bytes 10700172 | solution.py:125
  100.1 3.1 fusion.5
  103.6 3.0 fusion.1
  106.7 1.3 collective-permute-start
  109.4 2.5 collective-permute-done.1
  112.9 6.9 %conditional.5 = (bf16[1,32,2048]{2,1,0:T(8,128)(2,1)S(1)}) conditional(s32[]{:T(128)} %convert_element_type.398, () %tuple.120, (bf16[1,32,2048]{2,1,0:T(8,128)(2,1)S(1)}, pred[1,32,2048]{2,1,0:T(8,128)(4,1)S(1)}, bf16[1,32,2048]{2,1,0:T(8,128)(2,1)S(1)}, f32[1,2048]{1,0:T(1,128)S(1)}, bf16[2048,1024]{1,0:T(8,128)(2,1)}, ...), branch_computations={%region_1.1_spmd, %region_2.5_spmd} | conditional | flops 273973632 | bytes 10700172 | solution.py:125
  113.3 3.1 fusion.5
  116.8 3.0 fusion.1
  119.9 4.4 %collective-permute-start = (bf16[1,32,2048]{2,1,0:T(8,128)(2,1)S(1)}, bf16[1,32,2048]{2,1,0:T(8,128)(2,1)S(1)}, u32[]{:S(2)}, u32[]{:S(2)}) collective-permute-start(bf16[1,32,2048]{2,1,0:T(8,128)(2,1)S(1)} %get-tuple-element.1286), channel_id=1, source_target_pairs={{0,16},{1,17},{2,18},{3,19},{4,20},{5,21},{6,22},{7,23},{8,24},{9,... | collective-permute-start | bytes 393224 | tf_op jit(solution)/shard_map/while/body/eval_jaxpr/ppermute | solution.py:36
  125.7 2.5 collective-permute-done.1
  129.2 6.9 %conditional.5 = (bf16[1,32,2048]{2,1,0:T(8,128)(2,1)S(1)}) conditional(s32[]{:T(128)} %convert_element_type.398, () %tuple.120, (bf16[1,32,2048]{2,1,0:T(8,128)(2,1)S(1)}, pred[1,32,2048]{2,1,0:T(8,128)(4,1)S(1)}, bf16[1,32,2048]{2,1,0:T(8,128)(2,1)S(1)}, f32[1,2048]{1,0:T(1,128)S(1)}, bf16[2048,1024]{1,0:T(8,128)(2,1)}, ...), branch_computations={%region_1.1_spmd, %region_2.5_spmd} | conditional | flops 273973632 | bytes 10700172 | solution.py:125
  129.6 3.1 fusion.5
  133.1 3.0 fusion.1
  136.2 4.4 %collective-permute-start = (bf16[1,32,2048]{2,1,0:T(8,128)(2,1)S(1)}, bf16[1,32,2048]{2,1,0:T(8,128)(2,1)S(1)}, u32[]{:S(2)}, u32[]{:S(2)}) collective-permute-start(bf16[1,32,2048]{2,1,0:T(8,128)(2,1)S(1)} %get-tuple-element.1286), channel_id=1, source_target_pairs={{0,16},{1,17},{2,18},{3,19},{4,20},{5,21},{6,22},{7,23},{8,24},{9,... | collective-permute-start | bytes 393224 | tf_op jit(solution)/shard_map/while/body/eval_jaxpr/ppermute | solution.py:36
  142.0 2.5 collective-permute-done.1
  145.5 6.9 %conditional.5 = (bf16[1,32,2048]{2,1,0:T(8,128)(2,1)S(1)}) conditional(s32[]{:T(128)} %convert_element_type.398, () %tuple.120, (bf16[1,32,2048]{2,1,0:T(8,128)(2,1)S(1)}, pred[1,32,2048]{2,1,0:T(8,128)(4,1)S(1)}, bf16[1,32,2048]{2,1,0:T(8,128)(2,1)S(1)}, f32[1,2048]{1,0:T(1,128)S(1)}, bf16[2048,1024]{1,0:T(8,128)(2,1)}, ...), branch_computations={%region_1.1_spmd, %region_2.5_spmd} | conditional | flops 273973632 | bytes 10700172 | solution.py:125
  145.9 3.1 fusion.5
  149.4 3.0 fusion.1
  152.5 4.4 %collective-permute-start = (bf16[1,32,2048]{2,1,0:T(8,128)(2,1)S(1)}, bf16[1,32,2048]{2,1,0:T(8,128)(2,1)S(1)}, u32[]{:S(2)}, u32[]{:S(2)}) collective-permute-start(bf16[1,32,2048]{2,1,0:T(8,128)(2,1)S(1)} %get-tuple-element.1286), channel_id=1, source_target_pairs={{0,16},{1,17},{2,18},{3,19},{4,20},{5,21},{6,22},{7,23},{8,24},{9,... | collective-permute-start | bytes 393224 | tf_op jit(solution)/shard_map/while/body/eval_jaxpr/ppermute | solution.py:36
  156.9 1.3 collective-permute-start.1
  158.3 2.5 collective-permute-done.1
  161.9 11.3 %collective-permute-start = (bf16[1,32,2048]{2,1,0:T(8,128)(2,1)S(1)}, bf16[1,32,2048]{2,1,0:T(8,128)(2,1)S(1)}, u32[]{:S(2)}, u32[]{:S(2)}) collective-permute-start(bf16[1,32,2048]{2,1,0:T(8,128)(2,1)S(1)} %get-tuple-element.1286), channel_id=1, source_target_pairs={{0,16},{1,17},{2,18},{3,19},{4,20},{5,21},{6,22},{7,23},{8,24},{9,... | collective-permute-start | bytes 393224 | tf_op jit(solution)/shard_map/while/body/eval_jaxpr/ppermute | solution.py:36
  174.6 2.5 collective-permute-done.1
  177.2 197.1 %while.43 = (s32[]{:T(128)}, bf16[1,32,2048]{2,1,0:T(8,128)(2,1)S(1)}, bf16[1,32,2048]{2,1,0:T(8,128)(2,1)S(1)}, bf16[4,1,32,2048]{3,2,1,0:T(8,128)(2,1)S(1)}, f...) while((s32[]{:T(128)}, ...), condition=%wide.region_19.20_spmd.clone, body=%wide.region_7.19_spmd.clone.sunk | while | flops 417616544 | bytes 54149656 | solution.py:172
  180.0 30.0 %psum.15 = f32[2048]{0:T(1024)S(1)} all-reduce(f32[2048]{0:T(1024)S(1)} %get-tuple-element.1162), channel_id=1, replica_groups=mesh['section'=2,'fsdp'=16] {'fsdp'}, use_global_device_ids=true, to_apply=%region_18.18 | all-reduce | flops 2048 | bytes 16384 | tf_op jit(solution)/shard_map/while/body/eval_jaxpr/psum | solution.py:168
  210.1 8.2 %conditional.6 = (bf16[1,32,2048]{2,1,0:T(8,128)(2,1)S(1)}, bf16[1,32,2048]{2,1,0:T(8,128)(2,1)S(1)}, f32[2048]{0:T(1024)S(1)}) conditional(s32[]{:T(128)} %convert_element_type.399, () %tuple.124, (bf16[4,1,32,2048]{3,2,1,0:T(8,128)(2,1)S(1)}, s32[]{:T(128)}, pred[1,32,2048]{2,1,0:T(32,128)(4,1)S(1)}, bf16[1,32,2048]{2,1,0:T(8,128)(2,1)S(1)}, ...), branch_computations={%region_8.8_spmd, %region_9.17_spmd} | conditional | flops 417282720 | bytes 51683432 | solution.py:162
  210.5 3.3 fusion.38
  214.0 1.3 fusion.37
  216.5 1.5 fusion.50
  221.1 30.0 %psum.15 = f32[2048]{0:T(1024)S(1)} all-reduce(f32[2048]{0:T(1024)S(1)} %get-tuple-element.1162), channel_id=1, replica_groups=mesh['section'=2,'fsdp'=16] {'fsdp'}, use_global_device_ids=true, to_apply=%region_18.18 | all-reduce | flops 2048 | bytes 16384 | tf_op jit(solution)/shard_map/while/body/eval_jaxpr/psum | solution.py:168
  251.2 8.2 %conditional.6 = (bf16[1,32,2048]{2,1,0:T(8,128)(2,1)S(1)}, bf16[1,32,2048]{2,1,0:T(8,128)(2,1)S(1)}, f32[2048]{0:T(1024)S(1)}) conditional(s32[]{:T(128)} %convert_element_type.399, () %tuple.124, (bf16[4,1,32,2048]{3,2,1,0:T(8,128)(2,1)S(1)}, s32[]{:T(128)}, pred[1,32,2048]{2,1,0:T(32,128)(4,1)S(1)}, bf16[1,32,2048]{2,1,0:T(8,128)(2,1)S(1)}, ...), branch_computations={%region_8.8_spmd, %region_9.17_spmd} | conditional | flops 417282720 | bytes 51683432 | solution.py:162
  251.6 3.2 fusion.38
  255.0 1.3 fusion.37
  257.6 1.5 fusion.50
  262.1 30.0 %psum.15 = f32[2048]{0:T(1024)S(1)} all-reduce(f32[2048]{0:T(1024)S(1)} %get-tuple-element.1162), channel_id=1, replica_groups=mesh['section'=2,'fsdp'=16] {'fsdp'}, use_global_device_ids=true, to_apply=%region_18.18 | all-reduce | flops 2048 | bytes 16384 | tf_op jit(solution)/shard_map/while/body/eval_jaxpr/psum | solution.py:168
  292.2 8.2 %conditional.6 = (bf16[1,32,2048]{2,1,0:T(8,128)(2,1)S(1)}, bf16[1,32,2048]{2,1,0:T(8,128)(2,1)S(1)}, f32[2048]{0:T(1024)S(1)}) conditional(s32[]{:T(128)} %convert_element_type.399, () %tuple.124, (bf16[4,1,32,2048]{3,2,1,0:T(8,128)(2,1)S(1)}, s32[]{:T(128)}, pred[1,32,2048]{2,1,0:T(32,128)(4,1)S(1)}, bf16[1,32,2048]{2,1,0:T(8,128)(2,1)S(1)}, ...), branch_computations={%region_8.8_spmd, %region_9.17_spmd} | conditional | flops 417282720 | bytes 51683432 | solution.py:162
  292.6 3.3 fusion.38
  296.1 1.3 fusion.37
  298.7 1.5 fusion.50
  303.2 30.0 %psum.15 = f32[2048]{0:T(1024)S(1)} all-reduce(f32[2048]{0:T(1024)S(1)} %get-tuple-element.1162), channel_id=1, replica_groups=mesh['section'=2,'fsdp'=16] {'fsdp'}, use_global_device_ids=true, to_apply=%region_18.18 | all-reduce | flops 2048 | bytes 16384 | tf_op jit(solution)/shard_map/while/body/eval_jaxpr/psum | solution.py:168
  333.3 8.2 %conditional.6 = (bf16[1,32,2048]{2,1,0:T(8,128)(2,1)S(1)}, bf16[1,32,2048]{2,1,0:T(8,128)(2,1)S(1)}, f32[2048]{0:T(1024)S(1)}) conditional(s32[]{:T(128)} %convert_element_type.399, () %tuple.124, (bf16[4,1,32,2048]{3,2,1,0:T(8,128)(2,1)S(1)}, s32[]{:T(128)}, pred[1,32,2048]{2,1,0:T(32,128)(4,1)S(1)}, bf16[1,32,2048]{2,1,0:T(8,128)(2,1)S(1)}, ...), branch_computations={%region_8.8_spmd, %region_9.17_spmd} | conditional | flops 417282720 | bytes 51683432 | solution.py:162
  333.7 3.3 fusion.38
  337.2 1.3 fusion.37
  339.7 1.5 fusion.50
  344.3 30.0 %psum.15 = f32[2048]{0:T(1024)S(1)} all-reduce(f32[2048]{0:T(1024)S(1)} %get-tuple-element.1162), channel_id=1, replica_groups=mesh['section'=2,'fsdp'=16] {'fsdp'}, use_global_device_ids=true, to_apply=%region_18.18 | all-reduce | flops 2048 | bytes 16384 | tf_op jit(solution)/shard_map/while/body/eval_jaxpr/psum | solution.py:168
  (310 shorter events, 46.6 us)
Async XLA Ops:
  7.2 72.1 %copy-start = (bf16[16,2048]{1,0:T(8,128)(2,1)S(1)}, bf16[16,2048]{1,0:T(8,128)(2,1)}, u32[]{:S(2)}) copy-start(bf16[16,2048]{1,0:T(8,128)(2,1)} %param.19) | copy-start | bytes 196612
  7.2 83.1 %copy-start.7 = (bf16[1,128,1024]{2,1,0:T(8,128)(2,1)S(1)}, bf16[1,128,1024]{2,1,0:T(8,128)(2,1)}, u32[]{:S(2)}) copy-start(bf16[1,128,1024]{2,1,0:T(8,128)(2,1)} %param.20) | copy-start | bytes 786436
  7.2 91.2 %all-gather.2.cloned.1.call-start = ((), (), s32[]{:S(2)}) async-start(), calls=%async_computation | async-start | bytes 4456448 | tf_op jit(solution)/shard_map/all_gather | solution.py:87
  7.9 9.8 %collective-permute-start.4 = (bf16[1,128,1024]{2,1,0:T(8,128)(2,1)}, bf16[1,128,1024]{2,1,0:T(8,128)(2,1)S(1)}, u32[]{:S(2)}, u32[]{:S(2)}) collective-permute-start(bf16[1,128,1024]{2,1,0:T(8,128)(2,1)} %param.20), channel_id=1, source_target_pairs={{0,1},{1,2},{2,3},{3,4},{4,5},{5,6},{6,7},{7,8},{8,9},{9,10},{10,1... | collective-permute-start | bytes 786440 | tf_op jit(solution)/shard_map/ppermute | solution.py:24
  17.7 8.7 %collective-permute-start.5 = (bf16[1,128,1024]{2,1,0:T(8,128)(2,1)S(1)}, bf16[1,128,1024]{2,1,0:T(8,128)(2,1)S(1)}, u32[]{:S(2)}, u32[]{:S(2)}) collective-permute-start(bf16[1,128,1024]{2,1,0:T(8,128)(2,1)S(1)} %collective-permute-done.4), channel_id=1, source_target_pairs={{0,1},{1,2},{2,3},{3,4},{4,5},{5,6},{6,7},{7,8},{8,9},{9,10},{10,1... | collective-permute-start | bytes 786440 | tf_op jit(solution)/shard_map/ppermute | solution.py:24
  17.7 9.6 %collective-permute-start.12 = (bf16[1,128,1024]{2,1,0:T(8,128)(2,1)}, bf16[1,128,1024]{2,1,0:T(8,128)(2,1)S(1)}, u32[]{:S(2)}, u32[]{:S(2)}) collective-permute-start(bf16[1,128,1024]{2,1,0:T(8,128)(2,1)} %param.20), channel_id=1, source_target_pairs={{1,0},{2,1},{3,2},{4,3},{5,4},{6,5},{7,6},{8,7},{9,8},{10,9},{11,1... | collective-permute-start | bytes 786440 | tf_op jit(solution)/shard_map/ppermute | solution.py:26
  26.4 10.0 %collective-permute-start.6 = (bf16[1,128,1024]{2,1,0:T(8,128)(2,1)S(1)}, bf16[1,128,1024]{2,1,0:T(8,128)(2,1)S(1)}, u32[]{:S(2)}, u32[]{:S(2)}) collective-permute-start(bf16[1,128,1024]{2,1,0:T(8,128)(2,1)S(1)} %collective-permute-done.5), channel_id=1, source_target_pairs={{0,1},{1,2},{2,3},{3,4},{4,5},{5,6},{6,7},{7,8},{8,9},{9,10},{10,1... | collective-permute-start | bytes 786440 | tf_op jit(solution)/shard_map/ppermute | solution.py:24
  27.3 10.2 %collective-permute-start.13 = (bf16[1,128,1024]{2,1,0:T(8,128)(2,1)S(1)}, bf16[1,128,1024]{2,1,0:T(8,128)(2,1)S(1)}, u32[]{:S(2)}, u32[]{:S(2)}) collective-permute-start(bf16[1,128,1024]{2,1,0:T(8,128)(2,1)S(1)} %collective-permute-done.12), channel_id=1, source_target_pairs={{1,0},{2,1},{3,2},{4,3},{5,4},{6,5},{7,6},{8,7},{9,8},{10,9},{11,1... | collective-permute-start | bytes 786440 | tf_op jit(solution)/shard_map/ppermute | solution.py:26
  36.4 8.6 %collective-permute-start.7 = (bf16[1,128,1024]{2,1,0:T(8,128)(2,1)S(1)}, bf16[1,128,1024]{2,1,0:T(8,128)(2,1)S(1)}, u32[]{:S(2)}, u32[]{:S(2)}) collective-permute-start(bf16[1,128,1024]{2,1,0:T(8,128)(2,1)S(1)} %collective-permute-done.6), channel_id=1, source_target_pairs={{0,1},{1,2},{2,3},{3,4},{4,5},{5,6},{6,7},{7,8},{8,9},{9,10},{10,1... | collective-permute-start | bytes 786440 | tf_op jit(solution)/shard_map/ppermute | solution.py:24
  37.5 13.3 %collective-permute-start.14 = (bf16[1,128,1024]{2,1,0:T(8,128)(2,1)S(1)}, bf16[1,128,1024]{2,1,0:T(8,128)(2,1)S(1)}, u32[]{:S(2)}, u32[]{:S(2)}) collective-permute-start(bf16[1,128,1024]{2,1,0:T(8,128)(2,1)S(1)} %collective-permute-done.13), channel_id=1, source_target_pairs={{1,0},{2,1},{3,2},{4,3},{5,4},{6,5},{7,6},{8,7},{9,8},{10,9},{11,1... | collective-permute-start | bytes 786440 | tf_op jit(solution)/shard_map/ppermute | solution.py:26
  45.0 14.1 %collective-permute-start.8 = (bf16[1,128,1024]{2,1,0:T(8,128)(2,1)S(1)}, bf16[1,128,1024]{2,1,0:T(8,128)(2,1)S(1)}, u32[]{:S(2)}, u32[]{:S(2)}) collective-permute-start(bf16[1,128,1024]{2,1,0:T(8,128)(2,1)S(1)} %collective-permute-done.7), channel_id=1, source_target_pairs={{0,1},{1,2},{2,3},{3,4},{4,5},{5,6},{6,7},{7,8},{8,9},{9,10},{10,1... | collective-permute-start | bytes 786440 | tf_op jit(solution)/shard_map/ppermute | solution.py:24
  50.8 8.9 %collective-permute-start.15 = (bf16[1,128,1024]{2,1,0:T(8,128)(2,1)S(1)}, bf16[1,128,1024]{2,1,0:T(8,128)(2,1)S(1)}, u32[]{:S(2)}, u32[]{:S(2)}) collective-permute-start(bf16[1,128,1024]{2,1,0:T(8,128)(2,1)S(1)} %collective-permute-done.14), channel_id=1, source_target_pairs={{1,0},{2,1},{3,2},{4,3},{5,4},{6,5},{7,6},{8,7},{9,8},{10,9},{11,1... | collective-permute-start | bytes 786440 | tf_op jit(solution)/shard_map/ppermute | solution.py:26
  59.0 8.6 %collective-permute-start.9 = (bf16[1,128,1024]{2,1,0:T(8,128)(2,1)S(1)}, bf16[1,128,1024]{2,1,0:T(8,128)(2,1)S(1)}, u32[]{:S(2)}, u32[]{:S(2)}) collective-permute-start(bf16[1,128,1024]{2,1,0:T(8,128)(2,1)S(1)} %collective-permute-done.8), channel_id=1, source_target_pairs={{0,1},{1,2},{2,3},{3,4},{4,5},{5,6},{6,7},{7,8},{8,9},{9,10},{10,1... | collective-permute-start | bytes 786440 | tf_op jit(solution)/shard_map/ppermute | solution.py:24
  59.8 13.8 %collective-permute-start.16 = (bf16[1,128,1024]{2,1,0:T(8,128)(2,1)S(1)}, bf16[1,128,1024]{2,1,0:T(8,128)(2,1)S(1)}, u32[]{:S(2)}, u32[]{:S(2)}) collective-permute-start(bf16[1,128,1024]{2,1,0:T(8,128)(2,1)S(1)} %collective-permute-done.15), channel_id=1, source_target_pairs={{1,0},{2,1},{3,2},{4,3},{5,4},{6,5},{7,6},{8,7},{9,8},{10,9},{11,1... | collective-permute-start | bytes 786440 | tf_op jit(solution)/shard_map/ppermute | solution.py:26
  67.6 11.7 %copy-start.8 = (bf16[1,128,1024]{2,1,0:T(8,128)(2,1)}, bf16[1,128,1024]{2,1,0:T(8,128)(2,1)S(1)}, u32[]{:S(2)}) copy-start(bf16[1,128,1024]{2,1,0:T(8,128)(2,1)S(1)} %collective-permute-done.9) | copy-start | bytes 786436
  67.6 10.8 %collective-permute-start.10 = (bf16[1,128,1024]{2,1,0:T(8,128)(2,1)S(1)}, bf16[1,128,1024]{2,1,0:T(8,128)(2,1)}, u32[]{:S(2)}, u32[]{:S(2)}) collective-permute-start(bf16[1,128,1024]{2,1,0:T(8,128)(2,1)S(1)} %collective-permute-done.9), channel_id=1, source_target_pairs={{0,1},{1,2},{2,3},{3,4},{4,5},{5,6},{6,7},{7,8},{8,9},{9,10},{10,1... | collective-permute-start | bytes 786440 | tf_op jit(solution)/shard_map/ppermute | solution.py:24
  73.5 8.5 %collective-permute-start.17 = (bf16[1,128,1024]{2,1,0:T(8,128)(2,1)S(1)}, bf16[1,128,1024]{2,1,0:T(8,128)(2,1)}, u32[]{:S(2)}, u32[]{:S(2)}) collective-permute-start(bf16[1,128,1024]{2,1,0:T(8,128)(2,1)S(1)} %collective-permute-done.16), channel_id=1, source_target_pairs={{1,0},{2,1},{3,2},{4,3},{5,4},{6,5},{7,6},{8,7},{9,8},{10,9},{11,1... | collective-permute-start | bytes 786440 | tf_op jit(solution)/shard_map/ppermute | solution.py:26
  78.4 8.8 %collective-permute-start.11 = (bf16[1,128,1024]{2,1,0:T(8,128)(2,1)}, bf16[1,128,1024]{2,1,0:T(8,128)(2,1)}, u32[]{:S(2)}, u32[]{:S(2)}) collective-permute-start(bf16[1,128,1024]{2,1,0:T(8,128)(2,1)} %collective-permute-done.10), channel_id=1, source_target_pairs={{0,1},{1,2},{2,3},{3,4},{4,5},{5,6},{6,7},{7,8},{8,9},{9,10},{10,1... | collective-permute-start | bytes 786440 | tf_op jit(solution)/shard_map/ppermute | solution.py:24
  82.0 9.4 %collective-permute-start.18 = (bf16[1,128,1024]{2,1,0:T(8,128)(2,1)}, bf16[1,128,1024]{2,1,0:T(8,128)(2,1)S(1)}, u32[]{:S(2)}, u32[]{:S(2)}) collective-permute-start(bf16[1,128,1024]{2,1,0:T(8,128)(2,1)} %collective-permute-done.17), channel_id=1, source_target_pairs={{1,0},{2,1},{3,2},{4,3},{5,4},{6,5},{7,6},{8,7},{9,8},{10,9},{11,1... | collective-permute-start | bytes 786440 | tf_op jit(solution)/shard_map/ppermute | solution.py:26
  91.4 2.0 copy-start.4
  93.4 5.2 %copy-start.3 = (f32[1,2048]{1,0:T(1,128)S(1)}, f32[1,2048]{1,0:T(1,128)}, u32[]{:S(2)}) copy-start(f32[1,2048]{1,0:T(1,128)} %param.22) | copy-start | bytes 24580
  93.4 5.2 %copy-start.10 = (s32[4,1,32]{2,1,0:T(1,128)S(1)}, s32[4,1,32]{2,1,0:T(1,128)}, u32[]{:S(2)}) copy-start(s32[4,1,32]{2,1,0:T(1,128)} %param.17) | copy-start | bytes 1540
  98.6 78.6 %copy-start.5 = (bf16[4,1,32,2048]{3,2,1,0:T(8,128)(2,1)S(1)}, bf16[4,1,32,2048]{3,2,1,0:T(8,128)(2,1)}, u32[]{:S(2)}) copy-start(bf16[4,1,32,2048]{3,2,1,0:T(8,128)(2,1)} %param.23) | copy-start | bytes 1572868
  106.7 5.2 %collective-permute-start = (bf16[1,32,2048]{2,1,0:T(8,128)(2,1)S(1)}, bf16[1,32,2048]{2,1,0:T(8,128)(2,1)S(1)}, u32[]{:S(2)}, u32[]{:S(2)}) collective-permute-start(bf16[1,32,2048]{2,1,0:T(8,128)(2,1)S(1)} %get-tuple-element.1286), channel_id=1, source_target_pairs={{0,16},{1,17},{2,18},{3,19},{4,20},{5,21},{6,22},{7,23},{8,24},{9,... | collective-permute-start | bytes 393224 | tf_op jit(solution)/shard_map/while/body/eval_jaxpr/ppermute | solution.py:36
  108.0 3.8 %collective-permute-start.1 = (bf16[1,32,2048]{2,1,0:T(8,128)(2,1)S(1)}, bf16[1,32,2048]{2,1,0:T(8,128)(2,1)S(1)}, u32[]{:S(2)}, u32[]{:S(2)}) collective-permute-start(bf16[1,32,2048]{2,1,0:T(8,128)(2,1)S(1)} %select_select_fusion.2), channel_id=1, source_target_pairs={{0,16},{1,17},{2,18},{3,19},{4,20},{5,21},{6,22},{7,23},{8,24},{9,... | collective-permute-start | bytes 393224 | tf_op jit(solution)/shard_map/while/body/eval_jaxpr/ppermute | solution.py:36
  119.9 8.3 %collective-permute-start = (bf16[1,32,2048]{2,1,0:T(8,128)(2,1)S(1)}, bf16[1,32,2048]{2,1,0:T(8,128)(2,1)S(1)}, u32[]{:S(2)}, u32[]{:S(2)}) collective-permute-start(bf16[1,32,2048]{2,1,0:T(8,128)(2,1)S(1)} %get-tuple-element.1286), channel_id=1, source_target_pairs={{0,16},{1,17},{2,18},{3,19},{4,20},{5,21},{6,22},{7,23},{8,24},{9,... | collective-permute-start | bytes 393224 | tf_op jit(solution)/shard_map/while/body/eval_jaxpr/ppermute | solution.py:36
  124.3 3.8 %collective-permute-start.1 = (bf16[1,32,2048]{2,1,0:T(8,128)(2,1)S(1)}, bf16[1,32,2048]{2,1,0:T(8,128)(2,1)S(1)}, u32[]{:S(2)}, u32[]{:S(2)}) collective-permute-start(bf16[1,32,2048]{2,1,0:T(8,128)(2,1)S(1)} %select_select_fusion.2), channel_id=1, source_target_pairs={{0,16},{1,17},{2,18},{3,19},{4,20},{5,21},{6,22},{7,23},{8,24},{9,... | collective-permute-start | bytes 393224 | tf_op jit(solution)/shard_map/while/body/eval_jaxpr/ppermute | solution.py:36
  136.2 8.3 %collective-permute-start = (bf16[1,32,2048]{2,1,0:T(8,128)(2,1)S(1)}, bf16[1,32,2048]{2,1,0:T(8,128)(2,1)S(1)}, u32[]{:S(2)}, u32[]{:S(2)}) collective-permute-start(bf16[1,32,2048]{2,1,0:T(8,128)(2,1)S(1)} %get-tuple-element.1286), channel_id=1, source_target_pairs={{0,16},{1,17},{2,18},{3,19},{4,20},{5,21},{6,22},{7,23},{8,24},{9,... | collective-permute-start | bytes 393224 | tf_op jit(solution)/shard_map/while/body/eval_jaxpr/ppermute | solution.py:36
  140.6 3.8 %collective-permute-start.1 = (bf16[1,32,2048]{2,1,0:T(8,128)(2,1)S(1)}, bf16[1,32,2048]{2,1,0:T(8,128)(2,1)S(1)}, u32[]{:S(2)}, u32[]{:S(2)}) collective-permute-start(bf16[1,32,2048]{2,1,0:T(8,128)(2,1)S(1)} %select_select_fusion.2), channel_id=1, source_target_pairs={{0,16},{1,17},{2,18},{3,19},{4,20},{5,21},{6,22},{7,23},{8,24},{9,... | collective-permute-start | bytes 393224 | tf_op jit(solution)/shard_map/while/body/eval_jaxpr/ppermute | solution.py:36
  152.5 8.3 %collective-permute-start = (bf16[1,32,2048]{2,1,0:T(8,128)(2,1)S(1)}, bf16[1,32,2048]{2,1,0:T(8,128)(2,1)S(1)}, u32[]{:S(2)}, u32[]{:S(2)}) collective-permute-start(bf16[1,32,2048]{2,1,0:T(8,128)(2,1)S(1)} %get-tuple-element.1286), channel_id=1, source_target_pairs={{0,16},{1,17},{2,18},{3,19},{4,20},{5,21},{6,22},{7,23},{8,24},{9,... | collective-permute-start | bytes 393224 | tf_op jit(solution)/shard_map/while/body/eval_jaxpr/ppermute | solution.py:36
  156.9 3.8 %collective-permute-start.1 = (bf16[1,32,2048]{2,1,0:T(8,128)(2,1)S(1)}, bf16[1,32,2048]{2,1,0:T(8,128)(2,1)S(1)}, u32[]{:S(2)}, u32[]{:S(2)}) collective-permute-start(bf16[1,32,2048]{2,1,0:T(8,128)(2,1)S(1)} %select_select_fusion.2), channel_id=1, source_target_pairs={{0,16},{1,17},{2,18},{3,19},{4,20},{5,21},{6,22},{7,23},{8,24},{9,... | collective-permute-start | bytes 393224 | tf_op jit(solution)/shard_map/while/body/eval_jaxpr/ppermute | solution.py:36
  161.9 15.2 %collective-permute-start = (bf16[1,32,2048]{2,1,0:T(8,128)(2,1)S(1)}, bf16[1,32,2048]{2,1,0:T(8,128)(2,1)S(1)}, u32[]{:S(2)}, u32[]{:S(2)}) collective-permute-start(bf16[1,32,2048]{2,1,0:T(8,128)(2,1)S(1)} %get-tuple-element.1286), channel_id=1, source_target_pairs={{0,16},{1,17},{2,18},{3,19},{4,20},{5,21},{6,22},{7,23},{8,24},{9,... | collective-permute-start | bytes 393224 | tf_op jit(solution)/shard_map/while/body/eval_jaxpr/ppermute | solution.py:36
  173.2 3.8 %collective-permute-start.1 = (bf16[1,32,2048]{2,1,0:T(8,128)(2,1)S(1)}, bf16[1,32,2048]{2,1,0:T(8,128)(2,1)S(1)}, u32[]{:S(2)}, u32[]{:S(2)}) collective-permute-start(bf16[1,32,2048]{2,1,0:T(8,128)(2,1)S(1)} %select_select_fusion.2), channel_id=1, source_target_pairs={{0,16},{1,17},{2,18},{3,19},{4,20},{5,21},{6,22},{7,23},{8,24},{9,... | collective-permute-start | bytes 393224 | tf_op jit(solution)/shard_map/while/body/eval_jaxpr/ppermute | solution.py:36
  177.3 32.7 %collective-permute-start.2 = (bf16[1,32,2048]{2,1,0:T(8,128)(2,1)S(1)}, bf16[1,32,2048]{2,1,0:T(8,128)(2,1)S(1)}, u32[]{:S(2)}, u32[]{:S(2)}) collective-permute-start(bf16[1,32,2048]{2,1,0:T(8,128)(2,1)S(1)} %get-tuple-element.1160), channel_id=1, source_target_pairs={{16,0},{17,1},{18,2},{19,3},{20,4},{21,5},{22,6},{23,7},{24,8},{25... | collective-permute-start | bytes 393224 | tf_op jit(solution)/shard_map/while/body/eval_jaxpr/ppermute | solution.py:36
  178.6 31.4 %collective-permute-start.3 = (bf16[1,32,2048]{2,1,0:T(8,128)(2,1)S(1)}, bf16[1,32,2048]{2,1,0:T(8,128)(2,1)S(1)}, u32[]{:S(2)}, u32[]{:S(2)}) collective-permute-start(bf16[1,32,2048]{2,1,0:T(8,128)(2,1)S(1)} %get-tuple-element.1161), channel_id=1, source_target_pairs={{16,0},{17,1},{18,2},{19,3},{20,4},{21,5},{22,6},{23,7},{24,8},{25... | collective-permute-start | bytes 393224 | tf_op jit(solution)/shard_map/while/body/eval_jaxpr/ppermute | solution.py:36
  210.1 3.8 %copy-start.2 = (bf16[1024,2048]{1,0:T(8,128)(2,1)S(1)}, bf16[1024,2048]{1,0:T(8,128)(2,1)}, u32[]{:S(2)}) copy-start(bf16[1024,2048]{1,0:T(8,128)(2,1)} %get-tuple-element.750) | copy-start | bytes 12582916 | tf_op jit(solution)/shard_map/while/body/eval_jaxpr/cond
  213.7 2.8 copy-start.1
  218.4 32.7 %collective-permute-start.2 = (bf16[1,32,2048]{2,1,0:T(8,128)(2,1)S(1)}, bf16[1,32,2048]{2,1,0:T(8,128)(2,1)S(1)}, u32[]{:S(2)}, u32[]{:S(2)}) collective-permute-start(bf16[1,32,2048]{2,1,0:T(8,128)(2,1)S(1)} %get-tuple-element.1160), channel_id=1, source_target_pairs={{16,0},{17,1},{18,2},{19,3},{20,4},{21,5},{22,6},{23,7},{24,8},{25... | collective-permute-start | bytes 393224 | tf_op jit(solution)/shard_map/while/body/eval_jaxpr/ppermute | solution.py:36
  219.7 31.4 %collective-permute-start.3 = (bf16[1,32,2048]{2,1,0:T(8,128)(2,1)S(1)}, bf16[1,32,2048]{2,1,0:T(8,128)(2,1)S(1)}, u32[]{:S(2)}, u32[]{:S(2)}) collective-permute-start(bf16[1,32,2048]{2,1,0:T(8,128)(2,1)S(1)} %get-tuple-element.1161), channel_id=1, source_target_pairs={{16,0},{17,1},{18,2},{19,3},{20,4},{21,5},{22,6},{23,7},{24,8},{25... | collective-permute-start | bytes 393224 | tf_op jit(solution)/shard_map/while/body/eval_jaxpr/ppermute | solution.py:36
  251.2 3.8 %copy-start.2 = (bf16[1024,2048]{1,0:T(8,128)(2,1)S(1)}, bf16[1024,2048]{1,0:T(8,128)(2,1)}, u32[]{:S(2)}) copy-start(bf16[1024,2048]{1,0:T(8,128)(2,1)} %get-tuple-element.750) | copy-start | bytes 12582916 | tf_op jit(solution)/shard_map/while/body/eval_jaxpr/cond
  254.8 2.8 copy-start.1
  259.5 32.7 %collective-permute-start.2 = (bf16[1,32,2048]{2,1,0:T(8,128)(2,1)S(1)}, bf16[1,32,2048]{2,1,0:T(8,128)(2,1)S(1)}, u32[]{:S(2)}, u32[]{:S(2)}) collective-permute-start(bf16[1,32,2048]{2,1,0:T(8,128)(2,1)S(1)} %get-tuple-element.1160), channel_id=1, source_target_pairs={{16,0},{17,1},{18,2},{19,3},{20,4},{21,5},{22,6},{23,7},{24,8},{25... | collective-permute-start | bytes 393224 | tf_op jit(solution)/shard_map/while/body/eval_jaxpr/ppermute | solution.py:36
  260.8 31.4 %collective-permute-start.3 = (bf16[1,32,2048]{2,1,0:T(8,128)(2,1)S(1)}, bf16[1,32,2048]{2,1,0:T(8,128)(2,1)S(1)}, u32[]{:S(2)}, u32[]{:S(2)}) collective-permute-start(bf16[1,32,2048]{2,1,0:T(8,128)(2,1)S(1)} %get-tuple-element.1161), channel_id=1, source_target_pairs={{16,0},{17,1},{18,2},{19,3},{20,4},{21,5},{22,6},{23,7},{24,8},{25... | collective-permute-start | bytes 393224 | tf_op jit(solution)/shard_map/while/body/eval_jaxpr/ppermute | solution.py:36
  292.3 3.8 %copy-start.2 = (bf16[1024,2048]{1,0:T(8,128)(2,1)S(1)}, bf16[1024,2048]{1,0:T(8,128)(2,1)}, u32[]{:S(2)}) copy-start(bf16[1024,2048]{1,0:T(8,128)(2,1)} %get-tuple-element.750) | copy-start | bytes 12582916 | tf_op jit(solution)/shard_map/while/body/eval_jaxpr/cond
  295.9 2.8 copy-start.1
  300.5 32.7 %collective-permute-start.2 = (bf16[1,32,2048]{2,1,0:T(8,128)(2,1)S(1)}, bf16[1,32,2048]{2,1,0:T(8,128)(2,1)S(1)}, u32[]{:S(2)}, u32[]{:S(2)}) collective-permute-start(bf16[1,32,2048]{2,1,0:T(8,128)(2,1)S(1)} %get-tuple-element.1160), channel_id=1, source_target_pairs={{16,0},{17,1},{18,2},{19,3},{20,4},{21,5},{22,6},{23,7},{24,8},{25... | collective-permute-start | bytes 393224 | tf_op jit(solution)/shard_map/while/body/eval_jaxpr/ppermute | solution.py:36
  301.8 31.4 %collective-permute-start.3 = (bf16[1,32,2048]{2,1,0:T(8,128)(2,1)S(1)}, bf16[1,32,2048]{2,1,0:T(8,128)(2,1)S(1)}, u32[]{:S(2)}, u32[]{:S(2)}) collective-permute-start(bf16[1,32,2048]{2,1,0:T(8,128)(2,1)S(1)} %get-tuple-element.1161), channel_id=1, source_target_pairs={{16,0},{17,1},{18,2},{19,3},{20,4},{21,5},{22,6},{23,7},{24,8},{25... | collective-permute-start | bytes 393224 | tf_op jit(solution)/shard_map/while/body/eval_jaxpr/ppermute | solution.py:36
  333.3 3.8 %copy-start.2 = (bf16[1024,2048]{1,0:T(8,128)(2,1)S(1)}, bf16[1024,2048]{1,0:T(8,128)(2,1)}, u32[]{:S(2)}) copy-start(bf16[1024,2048]{1,0:T(8,128)(2,1)} %get-tuple-element.750) | copy-start | bytes 12582916 | tf_op jit(solution)/shard_map/while/body/eval_jaxpr/cond
  336.9 2.8 copy-start.1
  341.6 32.7 %collective-permute-start.2 = (bf16[1,32,2048]{2,1,0:T(8,128)(2,1)S(1)}, bf16[1,32,2048]{2,1,0:T(8,128)(2,1)S(1)}, u32[]{:S(2)}, u32[]{:S(2)}) collective-permute-start(bf16[1,32,2048]{2,1,0:T(8,128)(2,1)S(1)} %get-tuple-element.1160), channel_id=1, source_target_pairs={{16,0},{17,1},{18,2},{19,3},{20,4},{21,5},{22,6},{23,7},{24,8},{25... | collective-permute-start | bytes 393224 | tf_op jit(solution)/shard_map/while/body/eval_jaxpr/ppermute | solution.py:36
  342.9 31.4 %collective-permute-start.3 = (bf16[1,32,2048]{2,1,0:T(8,128)(2,1)S(1)}, bf16[1,32,2048]{2,1,0:T(8,128)(2,1)S(1)}, u32[]{:S(2)}, u32[]{:S(2)}) collective-permute-start(bf16[1,32,2048]{2,1,0:T(8,128)(2,1)S(1)} %get-tuple-element.1161), channel_id=1, source_target_pairs={{16,0},{17,1},{18,2},{19,3},{20,4},{21,5},{22,6},{23,7},{24,8},{25... | collective-permute-start | bytes 393224 | tf_op jit(solution)/shard_map/while/body/eval_jaxpr/ppermute | solution.py:36
  374.3 0.8 copy-start.6
  374.3 0.8 copy-start.9
Sparse Core Ops, SparseCore 0:
  10.2 68.1 all-gather.1
